TPU v7x, 256 devices: a whole 4x4x8 slice. The times are simulated.
256 devices in a mesh: expert: 8 (over z), mp: 32 (over x, y, core).
Axes of the slice: x: 4, y: 4, z: 8, core: 2. Of those that a mesh axis runs over, the one named last changes fastest.
Arguments:
- tokens: bfloat16 [4096, 2048], P('expert', 'mp'), may hold values from -6 to 6
- expert_route: int32 [4096, 2], P('expert'), may hold values from 0 to 7, all different within a row; in each aligned block of 512 rows (0 to 511, 512 to 1023, ...) at most 256 rows name the same one
- route_gate: float32 [4096, 2], P('expert'), may hold values from 0.05 to 1
- request_lengths: int32 [32], replicated, may hold values from 1 to 1024, 4096 in all
- request_adapter: int32 [32], replicated, may hold values from 0 to 63, as said below
- request_order: int32 [32], replicated, may hold values from 0 to 31, each once
- gate_weight: bfloat16 [8, 5632, 2048], P('expert', 'mp'), may hold values from -0.125 to 0.125
- up_weight: bfloat16 [8, 5632, 2048], P('expert', 'mp'), may hold values from -0.125 to 0.125
- down_weight: bfloat16 [8, 5632, 2048], P('expert', 'mp'), may hold values from -0.15625 to 0.15625
- adapter_in: bfloat16 [8, 1024, 2048], P('expert', 'mp'), may hold values from -0.125 to 0.125
- adapter_out: bfloat16 [8, 5632, 1024], P('expert', 'mp'), may hold values from -1.5 to 1.5
Outputs:
- mixed: bfloat16 [4096, 2048], P('expert', 'mp')
Inputs may be any that keep to these rules, and one draw needn't show every extreme that they name: `expert_route`: the two entries of a row differ; within each aligned block of 512 rows (the tokens held at one position along `expert`) no expert is named by more than 256 rows, and in some block some expert is named by exactly 256 rows. `request_lengths`: they sum to 4096; the largest is 1024. `request_order`: each request index appears once. `request_adapter`: exactly 16 different adapters appear.
All inputs are finite; a program needn't handle non-finite values.
Results may differ from a plain program's by a relative error of at most 0.035.
Values may be sent and summed in bfloat16 or wider, within the bound.
No kernel may reach another device: no remote copies, remote signals or barrier semaphores. Data moves between devices by JAX's collectives and lax.ppermute only.
A program may use at most 64 MiB of HBM per device.

v0:
```python
import jax
import jax.numpy as jnp
from jax import lax
from jax.sharding import PartitionSpec as P

RANK = 16
ADAPTERS = 64


def token_adapters(request_lengths, request_adapter, request_order, first_token, token_count):
    request_ids = jnp.arange(request_lengths.shape[0], dtype=jnp.int32)
    chosen = (request_order[:, None] == request_ids[None, :]).astype(jnp.int32)
    packed_lengths = jnp.sum(chosen * request_lengths[None, :], axis=1, dtype=jnp.int32)
    packed_adapters = jnp.sum(chosen * request_adapter[None, :], axis=1, dtype=jnp.int32)
    boundary = jnp.cumsum(packed_lengths, dtype=jnp.int32)
    positions = first_token + jnp.arange(token_count, dtype=jnp.int32)
    packed_index = jnp.sum(
        (boundary[None, :] <= positions[:, None]).astype(jnp.int32), axis=1, dtype=jnp.int32
    )
    matches = (packed_index[:, None] == request_ids[None, :]).astype(jnp.int32)
    return jnp.sum(matches * packed_adapters[None, :], axis=1, dtype=jnp.int32)


def expert_slots(routes, groups, capacity):
    flat_routes = routes.reshape(-1)
    one_hot = (flat_routes[:, None] == jnp.arange(groups, dtype=jnp.int32)[None, :]).astype(
        jnp.int32
    )
    before = jnp.cumsum(one_hot, axis=0, dtype=jnp.int32) - one_hot
    seat_index = jnp.sum(before * one_hot, axis=1, dtype=jnp.int32)
    return (flat_routes * capacity + seat_index).reshape(routes.shape)


def contract_last(left, right):
    return lax.dot_general(
        left, right, (((1,), (1,)), ((), ())), preferred_element_type=jnp.float32
    )


def on_device(
    tokens,
    expert_route,
    route_gate,
    request_lengths,
    request_adapter,
    request_order,
    gate_weight,
    up_weight,
    down_weight,
    adapter_in,
    adapter_out,
):
    tok_rows, local_feat = tokens.shape
    groups = lax.axis_size("expert")
    n_mp = lax.axis_size("mp")
    capacity = 4 * tok_rows // groups
    total_slots = groups * capacity
    source_group = lax.axis_index("expert")
    rank_w = adapter_in[0]
    rank_cols_w = lax.all_to_all(rank_w, "mp", split_axis=1, concat_axis=0, tiled=True)
    adapter_of = token_adapters(
        request_lengths, request_adapter, request_order, source_group * tok_rows, tok_rows
    )
    slot_index = expert_slots(expert_route, groups, capacity)
    flat_slots = slot_index.reshape(-1)
    flat_tokens = jnp.broadcast_to(
        jnp.arange(tok_rows, dtype=jnp.int32)[:, None], slot_index.shape
    ).reshape(-1)
    slot_token = jnp.zeros((total_slots,), jnp.int32).at[flat_slots].set(flat_tokens)
    filled = jnp.zeros((total_slots,), jnp.bool_).at[flat_slots].set(True)
    slot_adapter = jnp.where(filled, adapter_of[slot_token], -1)
    blank = jnp.zeros((), tokens.dtype)
    send_rows = jnp.where(filled[:, None], tokens[slot_token], blank)
    arrived_local = lax.all_to_all(send_rows, "expert", split_axis=0, concat_axis=0, tiled=True)
    arrived_adapter = lax.all_to_all(
        slot_adapter, "expert", split_axis=0, concat_axis=0, tiled=True
    )
    row_count = arrived_local.shape[0]
    part_all = contract_last(arrived_local, rank_cols_w)
    pick = (arrived_adapter[:, None] == jnp.arange(ADAPTERS, dtype=jnp.int32)[None, :]).astype(
        jnp.float32
    )
    part_rank = jnp.sum(part_all.reshape(row_count, ADAPTERS, RANK) * pick[:, :, None], axis=1)
    arrived = lax.all_gather(arrived_local, "mp", axis=1, tiled=True)
    parts = lax.all_gather(part_rank.astype(jnp.bfloat16), "mp", axis=0, tiled=False)
    rank = jnp.sum(parts.astype(jnp.float32), axis=0).astype(jnp.bfloat16)
    gate_pre = contract_last(arrived, gate_weight[0])
    up_base = contract_last(arrived, up_weight[0])
    chosen = pick.astype(jnp.bfloat16)
    expanded = (rank[:, None, :] * chosen[:, :, None]).reshape(row_count, ADAPTERS * RANK)
    up = up_base + contract_last(expanded, adapter_out[0])
    hidden = (jax.nn.silu(gate_pre) * up).astype(jnp.bfloat16)
    down_w = down_weight[0]
    scattered = lax.psum_scatter(
        lax.dot_general(
            down_w, hidden, (((0,), (1,)), ((), ())), preferred_element_type=jnp.float32
        ).astype(jnp.bfloat16),
        "mp",
        scatter_dimension=0,
        tiled=True,
    )
    returned = lax.all_to_all(scattered, "expert", split_axis=1, concat_axis=1, tiled=True)
    returned_rows = jnp.transpose(returned)
    picked = returned_rows[slot_index].astype(jnp.float32)
    mixed = jnp.sum(route_gate[:, :, None] * picked, axis=1)
    return mixed.astype(jnp.bfloat16)


def solution(mesh):
    in_specs = (
        P("expert", "mp"),
        P("expert", None),
        P("expert", None),
        P(),
        P(),
        P(),
        P("expert", "mp", None),
        P("expert", "mp", None),
        P("expert", "mp", None),
        P("expert", "mp", None),
        P("expert", "mp", None),
    )
    out_specs = P("expert", "mp")
    return jax.shard_map(
        on_device, mesh=mesh, in_specs=in_specs, out_specs=out_specs, check_vma=False
    )
```

profile of v0, /device:TPU:2, one launch (start us, length us, event | category | flops | bytes accessed | tf_op | source)
XLA Modules:
  0.0 353.5 jit_solution(11466283499831162084)
XLA Ops:
  7.8 2.3 reduce-window.18
  11.3 4.3 %scatter_custom_fusion.1 = s32[2048]{0:T(1024)S(1)} fusion(s32[1024]{0:T(1024)S(1)} %bitcast.81, s32[1024]{0:T(1024)S(1)} %reshape.215, s32[]{:T(128)} %constant.14.clone.1), kind=kCustom, calls=%fused_computation.50 | custom fusion | bytes 8196 | tf_op jit(solution)/shard_map/scatter | solution.py:69
  17.0 13.2 %gather_fusion.1 = s32[2048]{0:T(1024)S(1)} fusion(s32[512]{0:T(512)S(1)} %select_reduce_fusion, s32[2048]{0:T(1024)S(1)} %fusion.21), kind=kCustom, calls=%fused_computation.1 | custom fusion | bytes 24576 | tf_op jit(solution)/shard_map/gather | solution.py:71
  30.2 4.3 %scatter_custom_fusion = pred[2048]{0:T(1024)(128)(4,1)S(1)} fusion(s32[1024]{0:T(1024)S(1)} %bitcast.82, pred[1024]{0:T(1024)(128)(4,1)S(1)} %broadcast.114, pred[]{:T(512)} %constant.12.clone.1), kind=kCustom, calls=%fused_computation.52 | custom fusion | bytes 2049 | tf_op jit(solution)/shard_map/scatter | solution.py:70
  35.1 8.5 %all-to-all-start.2 = ((s32[8,256,1]{1,2,0:T(1,128)}), s32[8,256,1]{1,2,0:T(1,128)S(1)}, u32[]{:S(2)}, u32[]{:S(2)}) async-start(s32[8,256,1]{1,2,0:T(1,128)} %bitcast.9), calls=%async_computation.2 | async-start | bytes 16384 | tf_op jit(solution)/shard_map/all_to_all | solution.py:75
  43.8 6.2 %gather_fusion = bf16[2048,64]{1,0:T(8,128)(2,1)S(1)} fusion(bf16[512,64]{1,0:T(8,128)(2,1)S(1)} %copy.66, s32[2048]{0:T(1024)S(1)} %fusion.21), kind=kCustom, calls=%fused_computation | custom fusion | bytes 532480 | tf_op jit(solution)/shard_map/gather | solution.py:73
  51.4 7.6 %all-to-all-start.1 = ((bf16[32,2,1024]{2,1,0:T(2,128)(2,1)}), bf16[32,2,1024]{2,1,0:T(2,128)(2,1)S(1)}, u32[]{:S(2)}, u32[]{:S(2)}) async-start(bf16[32,2,1024]{2,1,0:T(2,128)(2,1)} %reshape.235), calls=%async_computation.1 | async-start | bytes 262144 | tf_op jit(solution)/shard_map/all_to_all | solution.py:60
  59.7 5.9 %all-to-all-done.1 = bf16[32,2,1024]{2,1,0:T(2,128)(2,1)S(1)} async-done(((bf16[32,2,1024]{2,1,0:T(2,128)(2,1)}), bf16[32,2,1024]{2,1,0:T(2,128)(2,1)S(1)}, u32[]{:S(2)}, u32[]{:S(2)}) %all-to-all-start.1) | async-done | bytes 131104 | tf_op jit(solution)/shard_map/all_to_all | solution.py:60
  65.6 7.2 %all-to-all-start = ((bf16[8,256,64]{1,2,0:T(8,128)(2,1)}), bf16[8,256,64]{1,2,0:T(8,128)(2,1)S(1)}, u32[]{:S(2)}, u32[]{:S(2)}) async-start(bf16[8,256,64]{1,2,0:T(8,128)(2,1)} %broadcast_select_fusion), calls=%async_computation | async-start | bytes 524288 | tf_op jit(solution)/shard_map/all_to_all | solution.py:74
  73.2 11.8 %all-to-all-done = bf16[8,256,64]{1,2,0:T(8,128)(2,1)S(1)} async-done(((bf16[8,256,64]{1,2,0:T(8,128)(2,1)}), bf16[8,256,64]{1,2,0:T(8,128)(2,1)S(1)}, u32[]{:S(2)}, u32[]{:S(2)}) %all-to-all-start) | async-done | bytes 262176 | tf_op jit(solution)/shard_map/all_to_all | solution.py:74
  85.3 1.9 multiply_reduce_fusion
  88.2 40.8 %all-gather.6.cloned.1.call-done = bf16[65536,16]{0,1:T(8,128)(2,1)} async-done(((bf16[2048,16]{0,1:T(8,128)(2,1)}), bf16[65536,16]{0,1:T(8,128)(2,1)}) %all-gather.6.cloned.1.call-update) | async-done | bytes 2097168 | tf_op jit(solution)/shard_map/all_gather | solution.py:85
  129.0 2.7 copy.80
  132.5 2.3 broadcast_multiply_fusion
  134.8 54.3 %all-gather.4.cloned.1.call-done = bf16[2048,2048]{0,1:T(8,128)(2,1)} async-done(((bf16[2048,64]{0,1:T(8,128)(2,1)}), bf16[2048,2048]{0,1:T(8,128)(2,1)}) %all-gather.4.cloned.1.call-update) | async-done | bytes 8388624 | tf_op jit(solution)/shard_map/all_gather | solution.py:84
  189.1 6.4 %fusion.6 = f32[2048,176]{0,1:T(8,128)} fusion(bf16[2048,2048]{0,1:T(8,128)(2,1)} %all-gather.4.cloned.1.call-done, bf16[1,176,2048]{2,1,0:T(8,128)(2,1)S(1)} %copy-done.5), kind=kOutput, calls=%fused_computation.17 | convolution fusion | flops 1476395008 | bytes 10551296 | tf_op jit(solution)/shard_map/dot_general | solution.py:35
  195.5 2.9 fusion.8
  198.4 9.7 %convert_bitcast_fusion = bf16[2048,2048]{0,1:T(8,128)(2,1)} fusion(f32[2048,176]{0,1:T(8,128)} %fusion.6, bf16[2048,1024]{0,1:T(8,128)(2,1)} %bitcast.69, f32[2048,176]{0,1:T(8,128)} %fusion.8, bf16[1,176,2048]{2,1,0:T(8,128)(2,1)S(1)} %copy-done, bf16[1,176,1024]{2,1,0:T(8,128)(2,1)S(1)} %copy-done.7), kind=kOutput, calls=%fused_computation.5 | convolution fusion | flops 2221309952 | bytes 16547840 | tf_op jit(solution)/shard_map/dot_general | solution.py:95
  208.0 12.3 %copy.76 = bf16[2048,2048]{1,0:T(8,128)(2,1)} copy(bf16[2048,2048]{0,1:T(8,128)(2,1)} %convert_bitcast_fusion) | data formatting | bytes 16777216
  220.4 99.9 %reduce-scatter.4.cloned.1.call-done = bf16[64,2048]{1,0:T(8,128)(2,1)} async-done(((bf16[2048,2048]{1,0:T(8,128)(2,1)}), bf16[64,2048]{1,0:T(8,128)(2,1)}) %reduce-scatter.4.cloned.1.call-update) | async-done | bytes 262160
  322.4 7.0 %all-to-all-start.3 = ((bf16[64,8,256]{2,0,1:T(8,128)(2,1)}), bf16[64,8,256]{2,0,1:T(8,128)(2,1)S(1)}, u32[]{:S(2)}, u32[]{:S(2)}) async-start(bf16[64,8,256]{2,0,1:T(8,128)(2,1)} %copy.73), calls=%async_computation.3 | async-start | bytes 524288 | tf_op jit(solution)/shard_map/all_to_all | solution.py:102
  329.8 10.1 %all-to-all-done.3 = bf16[64,8,256]{2,0,1:T(8,128)(2,1)S(1)} async-done(((bf16[64,8,256]{2,0,1:T(8,128)(2,1)}), bf16[64,8,256]{2,0,1:T(8,128)(2,1)S(1)}, u32[]{:S(2)}, u32[]{:S(2)}) %all-to-all-start.3) | async-done | bytes 262176 | tf_op jit(solution)/shard_map/all_to_all | solution.py:102
  340.2 3.2 gather_fusion.2
  343.4 2.8 fusion.11
  (67 shorter events, 12.4 us)
Async XLA Ops:
  6.5 191.8 %copy-start = (bf16[1,176,2048]{2,1,0:T(8,128)(2,1)S(1)}, bf16[1,176,2048]{2,1,0:T(8,128)(2,1)}, u32[]{:S(2)}) copy-start(bf16[1,176,2048]{2,1,0:T(8,128)(2,1)} %param.19) | copy-start | bytes 2162692
  16.9 26.7 %copy-start.2 = (bf16[512,64]{0,1:T(8,128)(2,1)S(1)}, bf16[512,64]{0,1:T(8,128)(2,1)}, u32[]{:S(2)}) copy-start(bf16[512,64]{0,1:T(8,128)(2,1)} %param.11) | copy-start | bytes 196612
  30.2 20.0 %copy-start.1 = (bf16[1,32,2048]{2,1,0:T(8,128)(2,1)S(1)}, bf16[1,32,2048]{2,1,0:T(8,128)(2,1)}, u32[]{:S(2)}) copy-start(bf16[1,32,2048]{2,1,0:T(8,128)(2,1)} %param.20) | copy-start | bytes 393220
  35.1 16.2 %all-to-all-start.2 = ((s32[8,256,1]{1,2,0:T(1,128)}), s32[8,256,1]{1,2,0:T(1,128)S(1)}, u32[]{:S(2)}, u32[]{:S(2)}) async-start(s32[8,256,1]{1,2,0:T(1,128)} %bitcast.9), calls=%async_computation.2 | async-start | bytes 16384 | tf_op jit(solution)/shard_map/all_to_all | solution.py:75
  51.4 14.2 %all-to-all-start.1 = ((bf16[32,2,1024]{2,1,0:T(2,128)(2,1)}), bf16[32,2,1024]{2,1,0:T(2,128)(2,1)S(1)}, u32[]{:S(2)}, u32[]{:S(2)}) async-start(bf16[32,2,1024]{2,1,0:T(2,128)(2,1)} %reshape.235), calls=%async_computation.1 | async-start | bytes 262144 | tf_op jit(solution)/shard_map/all_to_all | solution.py:60
  65.6 19.4 %all-to-all-start = ((bf16[8,256,64]{1,2,0:T(8,128)(2,1)}), bf16[8,256,64]{1,2,0:T(8,128)(2,1)S(1)}, u32[]{:S(2)}, u32[]{:S(2)}) async-start(bf16[8,256,64]{1,2,0:T(8,128)(2,1)} %broadcast_select_fusion), calls=%async_computation | async-start | bytes 524288 | tf_op jit(solution)/shard_map/all_to_all | solution.py:74
  72.8 56.2 %all-gather.6.cloned.1.call-start = ((), (), s32[]{:S(2)}) async-start(), calls=%async_computation.6 | async-start | bytes 2162688 | tf_op jit(solution)/shard_map/all_gather | solution.py:85
  87.2 101.9 %all-gather.4.cloned.1.call-start = ((), (), s32[]{:S(2)}) async-start(), calls=%async_computation.5 | async-start | bytes 8650752 | tf_op jit(solution)/shard_map/all_gather | solution.py:84
  88.0 232.3 %reduce-scatter.4.cloned.1.call-start = ((), (), s32[]{:S(2)}) async-start(), calls=%async_computation.7 | async-start | bytes 8650752
  131.8 57.3 %copy-start.5 = (bf16[1,176,2048]{2,1,0:T(8,128)(2,1)S(1)}, bf16[1,176,2048]{2,1,0:T(8,128)(2,1)}, u32[]{:S(2)}) copy-start(bf16[1,176,2048]{2,1,0:T(8,128)(2,1)} %param.18) | copy-start | bytes 2162692
  134.8 60.7 %copy-start.6 = (bf16[1,176,2048]{2,1,0:T(8,128)(2,1)S(1)}, bf16[1,176,2048]{2,1,0:T(8,128)(2,1)}, u32[]{:S(2)}) copy-start(bf16[1,176,2048]{2,1,0:T(8,128)(2,1)} %param.17) | copy-start | bytes 2162692
  189.1 6.4 %copy-start.4 = (bf16[2048,2048]{0,1:T(8,128)(2,1)S(1)}, bf16[2048,2048]{0,1:T(8,128)(2,1)}, u32[]{:S(2)}) copy-start(bf16[2048,2048]{0,1:T(8,128)(2,1)} %all-gather.4.cloned.1.call-done) | copy-start | bytes 25165828
  195.5 2.9 copy-start.7
  220.4 109.2 %copy-start.3 = (f32[512,2]{0,1:T(2,128)S(1)}, f32[512,2]{0,1:T(2,128)}, u32[]{:S(2)}) copy-start(f32[512,2]{0,1:T(2,128)} %param.13) | copy-start | bytes 12292
  322.4 17.5 %all-to-all-start.3 = ((bf16[64,8,256]{2,0,1:T(8,128)(2,1)}), bf16[64,8,256]{2,0,1:T(8,128)(2,1)S(1)}, u32[]{:S(2)}, u32[]{:S(2)}) async-start(bf16[64,8,256]{2,0,1:T(8,128)(2,1)} %copy.73), calls=%async_computation.3 | async-start | bytes 524288 | tf_op jit(solution)/shard_map/all_to_all | solution.py:102
Sparse Core Ops, SparseCore 0:
  87.3 41.6 all-gather.5
  131.6 57.4 all-gather.3
  220.5 99.7 reduce-scatter.3
where the time goes:
time: 354 us
  waiting for transfers between devices  223 us (63%)
  local copies, waits for them, and re-layouts  54.8 us (15%)
  starting transfers between devices  30.6 us (9%)
  matrix products  20.8 us (6%)
  between operations  13.4 us (4%)
  other arithmetic  11.1 us (3%)
    unnamed x4, waiting for transfers between devices  99.9 us
    all_gather x1, waiting for transfers between devices, on_device(): arrived = lax.all_gather(arrived_local, 'mp', axis=1, tiled=True)  54.3 us
    all_gather x1, waiting for transfers between devices, on_device(): lax.all_gather(part_rank.astype(jnp.bfloat16), 'mp', axis=0, tiled=False)  40.8 us
    unnamed x24, local copies, waits for them, and re-layouts  18.6 us
    gather x1, local copies, waits for them, and re-layouts, on_device(): slot_adapter = jnp.where(filled, adapter_of[slot_token], -1)  13.2 us
    all_to_all x1, waiting for transfers between devices, on_device(): lax.all_to_all(send_rows, 'expert', split_axis=0, concat_axis=0, tiled=True)  11.8 us
    dot_general x3, matrix products, contract_last(): lax.dot_general(left, right, (((1,), (1,)), ((), ())), preferred_element_...  11.1 us
    all_to_all x1, waiting for transfers between devices, on_device(): lax.all_to_all(scattered, 'expert', split_axis=1, concat_axis=1, tiled=True)  10.1 us
  transfers between devices with their start and end apart: 7, of which 6 were waited for; matrix products, arithmetic and copies ran while one was open for 4% of the time, Pallas kernels for 0%

commit v1 on v0

--- a/solution.py
+++ b/solution.py
@@ -81,7 +81,12 @@
         jnp.float32
     )
     part_rank = jnp.sum(part_all.reshape(row_count, ADAPTERS, RANK) * pick[:, :, None], axis=1)
-    arrived = lax.all_gather(arrived_local, "mp", axis=1, tiled=True)
+    panels = []
+    for _ in range(jax.lax.psum(1, "mp")):
+        panels.append(arrived_local)
+    heard = jnp.stack(panels)
+    after = jax.lax.all_to_all(heard, "mp", 0, 0)
+    arrived = jnp.concatenate(after, axis=1)
     parts = lax.all_gather(part_rank.astype(jnp.bfloat16), "mp", axis=0, tiled=False)
     rank = jnp.sum(parts.astype(jnp.float32), axis=0).astype(jnp.bfloat16)
     gate_pre = contract_last(arrived, gate_weight[0])

time: 354 us -> 384 us (1.085)
  waiting for transfers between devices: 223 us -> 242 us
  starting transfers between devices: 30.6 us -> 36.1 us
    all_gather x1, waiting for transfers between devices: 40.8 us -> 107 us  [on_device(): lax.all_gather(part_rank.astype(jnp.bfloat16), 'mp', axis=0, tiled=False)]
    all_gather x1 -> x0, waiting for transfers between devices: 54.3 us -> none  [on_device(): arrived = lax.all_gather(arrived_local, 'mp', axis=1, tiled=True)]
    unnamed x4 -> x3, waiting for transfers between devices: 99.9 us -> 107 us
    all_to_all x0 -> x1, starting transfers between devices: none -> 6.04 us  [on_device(): after = jax.lax.all_to_all(heard, 'mp', 0, 0)]
    another operation x1 -> x4, local copies, waits for them, and re-layouts: 0.09 us -> 4.51 us  [the longest x3 4.42 us: on_device(): heard = jnp.stack(panels)]
    unnamed x24 -> x22, local copies, waits for them, and re-layouts: 18.6 us -> 18.6 us
where the time goes in v1:
time: 384 us
  waiting for transfers between devices  242 us (63%)
  local copies, waits for them, and re-layouts  58.3 us (15%)
  starting transfers between devices  36.1 us (9%)
  matrix products  22.5 us (6%)
  between operations  13.7 us (4%)
  other arithmetic  11 us (3%)
    unnamed x3, waiting for transfers between devices  107 us
    all_gather x1, waiting for transfers between devices, on_device(): lax.all_gather(part_rank.astype(jnp.bfloat16), 'mp', axis=0, tiled=False)  107 us
    unnamed x22, local copies, waits for them, and re-layouts  18.6 us
    dot_general x3, matrix products, contract_last(): lax.dot_general(left, right, (((1,), (1,)), ((), ())), preferred_element_...  13.3 us
    gather x1, local copies, waits for them, and re-layouts, on_device(): slot_adapter = jnp.where(filled, adapter_of[slot_token], -1)  13.2 us
    all_to_all x1, waiting for transfers between devices, on_device(): lax.all_to_all(scattered, 'expert', split_axis=1, concat_axis=1, tiled=True)  10.1 us
    all_to_all x1, waiting for transfers between devices, on_device(): lax.all_to_all(send_rows, 'expert', split_axis=0, concat_axis=0, tiled=True)  10.1 us
    dot_general x1, matrix products, on_device(): lax.dot_general(down_w, hidden, (((0,), (1,)), ((), ())), preferred_eleme...  9.23 us
  transfers between devices with their start and end apart: 7, of which 6 were waited for; matrix products, arithmetic and copies ran while one was open for 4% of the time, Pallas kernels for 0%

profile of v1, /device:TPU:2, one launch (start us, length us, event | category | flops | bytes accessed | tf_op | source)
XLA Modules:
  0.0 383.5 jit_solution(14239159502898504249)
XLA Ops:
  7.8 2.3 reduce-window.18
  11.3 4.3 %scatter_custom_fusion.1 = s32[2048]{0:T(1024)S(1)} fusion(s32[1024]{0:T(1024)S(1)} %bitcast.84, s32[1024]{0:T(1024)S(1)} %reshape.226, s32[]{:T(128)} %constant.14.clone.1), kind=kCustom, calls=%fused_computation.50 | custom fusion | bytes 8196 | tf_op jit(solution)/shard_map/scatter | solution.py:69
  16.8 4.3 %scatter_custom_fusion = pred[2048]{0:T(1024)(128)(4,1)S(1)} fusion(s32[1024]{0:T(1024)S(1)} %bitcast.85, pred[1024]{0:T(1024)(128)(4,1)S(1)} %broadcast.115, pred[]{:T(512)} %constant.12.clone.1), kind=kCustom, calls=%fused_computation.52 | custom fusion | bytes 2049 | tf_op jit(solution)/shard_map/scatter | solution.py:70
  21.3 13.2 %gather_fusion.1 = s32[2048]{0:T(1024)S(1)} fusion(s32[512]{0:T(512)S(1)} %select_reduce_fusion, s32[2048]{0:T(1024)S(1)} %fusion.21), kind=kCustom, calls=%fused_computation.1 | custom fusion | bytes 24576 | tf_op jit(solution)/shard_map/gather | solution.py:71
  35.1 8.5 %all-to-all-start.3 = ((s32[8,256,1]{1,2,0:T(1,128)}), s32[8,256,1]{1,2,0:T(1,128)S(1)}, u32[]{:S(2)}, u32[]{:S(2)}) async-start(s32[8,256,1]{1,2,0:T(1,128)} %bitcast.12), calls=%async_computation.3 | async-start | bytes 16384 | tf_op jit(solution)/shard_map/all_to_all | solution.py:75
  43.8 6.2 %gather_fusion = bf16[2048,64]{1,0:T(8,128)(2,1)S(1)} fusion(bf16[512,64]{1,0:T(8,128)(2,1)S(1)} %copy.67, s32[2048]{0:T(1024)S(1)} %fusion.21), kind=kCustom, calls=%fused_computation | custom fusion | bytes 532480 | tf_op jit(solution)/shard_map/gather | solution.py:73
  51.3 6.7 %all-to-all-start = ((bf16[8,256,64]{1,2,0:T(8,128)(2,1)}), bf16[8,256,64]{1,2,0:T(8,128)(2,1)S(1)}, u32[]{:S(2)}, u32[]{:S(2)}) async-start(bf16[8,256,64]{1,2,0:T(8,128)(2,1)} %broadcast_select_fusion), calls=%async_computation | async-start | bytes 524288 | tf_op jit(solution)/shard_map/all_to_all | solution.py:74
  59.3 10.1 %all-to-all-done = bf16[8,256,64]{1,2,0:T(8,128)(2,1)S(1)} async-done(((bf16[8,256,64]{1,2,0:T(8,128)(2,1)}), bf16[8,256,64]{1,2,0:T(8,128)(2,1)S(1)}, u32[]{:S(2)}, u32[]{:S(2)}) %all-to-all-start) | async-done | bytes 262176 | tf_op jit(solution)/shard_map/all_to_all | solution.py:74
  69.4 7.6 %all-to-all-start.2 = ((bf16[32,2,1024]{2,1,0:T(2,128)(2,1)}), bf16[32,2,1024]{2,1,0:T(2,128)(2,1)S(1)}, u32[]{:S(2)}, u32[]{:S(2)}) async-start(bf16[32,2,1024]{2,1,0:T(2,128)(2,1)} %reshape.246), calls=%async_computation.2 | async-start | bytes 262144 | tf_op jit(solution)/shard_map/all_to_all | solution.py:60
  77.0 6.6 %all-to-all-done.2 = bf16[32,2,1024]{2,1,0:T(2,128)(2,1)S(1)} async-done(((bf16[32,2,1024]{2,1,0:T(2,128)(2,1)}), bf16[32,2,1024]{2,1,0:T(2,128)(2,1)S(1)}, u32[]{:S(2)}, u32[]{:S(2)}) %all-to-all-start.2) | async-done | bytes 131104 | tf_op jit(solution)/shard_map/all_to_all | solution.py:60
  83.6 4.3 %stack.5 = bf16[32,2048,64]{1,2,0:T(8,128)(2,1)} broadcast(bf16[2048,64]{0,1:T(8,128)(2,1)S(1)} %bitcast.77), dimensions={1,2} | broadcast | bytes 8650752 | tf_op jit(solution)/shard_map/stack | solution.py:87
  87.9 6.0 %all-to-all-start.1 = ((bf16[32,2048,64]{1,2,0:T(8,128)(2,1)}), bf16[32,2048,64]{1,2,0:T(8,128)(2,1)}, u32[]{:S(2)}, u32[]{:S(2)}) async-start(bf16[32,2048,64]{1,2,0:T(8,128)(2,1)} %stack.5), calls=%async_computation.1 | async-start | bytes 16777216 | tf_op jit(solution)/shard_map/all_to_all | solution.py:88
  96.7 107.2 %all-gather.3.cloned.1.call-done = bf16[65536,16]{0,1:T(8,128)(2,1)} async-done(((bf16[2048,16]{0,1:T(8,128)(2,1)}), bf16[65536,16]{0,1:T(8,128)(2,1)}) %all-gather.3.cloned.1.call-update) | async-done | bytes 2097168 | tf_op jit(solution)/shard_map/all_gather | solution.py:90
  204.0 2.7 copy.81
  207.4 2.3 broadcast_multiply_fusion
  209.7 5.1 %fusion.6 = f32[2048,176]{0,1:T(8,128)S(1)} fusion(bf16[2048,2048]{0,1:T(8,128)(2,1)} %bitcast.5, bf16[1,176,2048]{2,1,0:T(8,128)(2,1)S(1)} %copy-done.4), kind=kOutput, calls=%fused_computation.17 | convolution fusion | flops 1476395008 | bytes 10551296 | tf_op jit(solution)/shard_map/dot_general | solution.py:35
  214.8 6.3 %fusion.8 = f32[2048,176]{0,1:T(8,128)} fusion(bf16[2048,2048]{0,1:T(8,128)(2,1)} %bitcast.5, bf16[1,176,2048]{2,1,0:T(8,128)(2,1)S(1)} %copy-done.5), kind=kOutput, calls=%fused_computation.19 | convolution fusion | flops 1476395008 | bytes 10551296 | tf_op jit(solution)/shard_map/dot_general | solution.py:35
  221.2 9.2 %convert_bitcast_fusion = bf16[2048,2048]{0,1:T(8,128)(2,1)} fusion(f32[2048,176]{0,1:T(8,128)S(1)} %fusion.6, bf16[2048,1024]{0,1:T(8,128)(2,1)} %bitcast.72, f32[2048,176]{0,1:T(8,128)} %fusion.8, bf16[1,176,2048]{2,1,0:T(8,128)(2,1)S(1)} %copy-done, bf16[1,176,1024]{2,1,0:T(8,128)(2,1)S(1)} %copy-done.6), kind=kOutput, calls=%fused_computation.5 | convolution fusion | flops 2221309952 | bytes 16547840 | tf_op jit(solution)/shard_map/dot_general | solution.py:100
  230.4 12.3 %copy.77 = bf16[2048,2048]{1,0:T(8,128)(2,1)} copy(bf16[2048,2048]{0,1:T(8,128)(2,1)} %convert_bitcast_fusion) | data formatting | bytes 16777216
  242.8 107.2 %reduce-scatter.4.cloned.1.call-done = bf16[64,2048]{1,0:T(8,128)(2,1)} async-done(((bf16[2048,2048]{1,0:T(8,128)(2,1)}), bf16[64,2048]{1,0:T(8,128)(2,1)}) %reduce-scatter.4.cloned.1.call-update) | async-done | bytes 262160
  352.1 7.0 %all-to-all-start.4 = ((bf16[64,8,256]{2,0,1:T(8,128)(2,1)}), bf16[64,8,256]{2,0,1:T(8,128)(2,1)S(1)}, u32[]{:S(2)}, u32[]{:S(2)}) async-start(bf16[64,8,256]{2,0,1:T(8,128)(2,1)} %copy.74), calls=%async_computation.4 | async-start | bytes 524288 | tf_op jit(solution)/shard_map/all_to_all | solution.py:107
  359.5 10.1 %all-to-all-done.4 = bf16[64,8,256]{2,0,1:T(8,128)(2,1)S(1)} async-done(((bf16[64,8,256]{2,0,1:T(8,128)(2,1)}), bf16[64,8,256]{2,0,1:T(8,128)(2,1)S(1)}, u32[]{:S(2)}, u32[]{:S(2)}) %all-to-all-start.4) | async-done | bytes 262176 | tf_op jit(solution)/shard_map/all_to_all | solution.py:107
  369.9 3.2 gather_fusion.2
  373.1 2.8 fusion.11
  (65 shorter events, 14.0 us)
Async XLA Ops:
  6.5 214.6 %copy-start = (bf16[1,176,2048]{2,1,0:T(8,128)(2,1)S(1)}, bf16[1,176,2048]{2,1,0:T(8,128)(2,1)}, u32[]{:S(2)}) copy-start(bf16[1,176,2048]{2,1,0:T(8,128)(2,1)} %param.19) | copy-start | bytes 2162692
  21.3 22.3 %copy-start.2 = (bf16[512,64]{0,1:T(8,128)(2,1)S(1)}, bf16[512,64]{0,1:T(8,128)(2,1)}, u32[]{:S(2)}) copy-start(bf16[512,64]{0,1:T(8,128)(2,1)} %param.11) | copy-start | bytes 196612
  34.5 23.5 %copy-start.1 = (bf16[1,32,2048]{2,1,0:T(8,128)(2,1)S(1)}, bf16[1,32,2048]{2,1,0:T(8,128)(2,1)}, u32[]{:S(2)}) copy-start(bf16[1,32,2048]{2,1,0:T(8,128)(2,1)} %param.20) | copy-start | bytes 393220
  35.1 16.2 %all-to-all-start.3 = ((s32[8,256,1]{1,2,0:T(1,128)}), s32[8,256,1]{1,2,0:T(1,128)S(1)}, u32[]{:S(2)}, u32[]{:S(2)}) async-start(s32[8,256,1]{1,2,0:T(1,128)} %bitcast.12), calls=%async_computation.3 | async-start | bytes 16384 | tf_op jit(solution)/shard_map/all_to_all | solution.py:75
  51.3 18.1 %all-to-all-start = ((bf16[8,256,64]{1,2,0:T(8,128)(2,1)}), bf16[8,256,64]{1,2,0:T(8,128)(2,1)S(1)}, u32[]{:S(2)}, u32[]{:S(2)}) async-start(bf16[8,256,64]{1,2,0:T(8,128)(2,1)} %broadcast_select_fusion), calls=%async_computation | async-start | bytes 524288 | tf_op jit(solution)/shard_map/all_to_all | solution.py:74
  69.4 14.2 %all-to-all-start.2 = ((bf16[32,2,1024]{2,1,0:T(2,128)(2,1)}), bf16[32,2,1024]{2,1,0:T(2,128)(2,1)S(1)}, u32[]{:S(2)}, u32[]{:S(2)}) async-start(bf16[32,2,1024]{2,1,0:T(2,128)(2,1)} %reshape.246), calls=%async_computation.2 | async-start | bytes 262144 | tf_op jit(solution)/shard_map/all_to_all | solution.py:60
  87.9 121.8 %all-to-all-start.1 = ((bf16[32,2048,64]{1,2,0:T(8,128)(2,1)}), bf16[32,2048,64]{1,2,0:T(8,128)(2,1)}, u32[]{:S(2)}, u32[]{:S(2)}) async-start(bf16[32,2048,64]{1,2,0:T(8,128)(2,1)} %stack.5), calls=%async_computation.1 | async-start | bytes 16777216 | tf_op jit(solution)/shard_map/all_to_all | solution.py:88
  94.0 110.0 %all-gather.3.cloned.1.call-start = ((), (), s32[]{:S(2)}) async-start(), calls=%async_computation.6 | async-start | bytes 2162688 | tf_op jit(solution)/shard_map/all_gather | solution.py:90
  96.5 253.5 %reduce-scatter.4.cloned.1.call-start = ((), (), s32[]{:S(2)}) async-start(), calls=%async_computation.7 | async-start | bytes 8650752
  206.7 3.0 copy-start.4
  209.7 5.1 %copy-start.5 = (bf16[1,176,2048]{2,1,0:T(8,128)(2,1)S(1)}, bf16[1,176,2048]{2,1,0:T(8,128)(2,1)}, u32[]{:S(2)}) copy-start(bf16[1,176,2048]{2,1,0:T(8,128)(2,1)} %param.17) | copy-start | bytes 2162692
  214.8 6.3 %copy-start.6 = (bf16[1,176,1024]{2,1,0:T(8,128)(2,1)S(1)}, bf16[1,176,1024]{2,1,0:T(8,128)(2,1)}, u32[]{:S(2)}) copy-start(bf16[1,176,1024]{2,1,0:T(8,128)(2,1)} %param.21) | copy-start | bytes 1081348
  242.7 116.6 %copy-start.3 = (f32[512,2]{0,1:T(2,128)S(1)}, f32[512,2]{0,1:T(2,128)}, u32[]{:S(2)}) copy-start(f32[512,2]{0,1:T(2,128)} %param.13) | copy-start | bytes 12292
  352.1 17.5 %all-to-all-start.4 = ((bf16[64,8,256]{2,0,1:T(8,128)(2,1)}), bf16[64,8,256]{2,0,1:T(8,128)(2,1)S(1)}, u32[]{:S(2)}, u32[]{:S(2)}) async-start(bf16[64,8,256]{2,0,1:T(8,128)(2,1)} %copy.74), calls=%async_computation.4 | async-start | bytes 524288 | tf_op jit(solution)/shard_map/all_to_all | solution.py:107
Sparse Core Ops, SparseCore 0:
  97.4 106.5 all-gather.2
  242.9 107.0 reduce-scatter.3
